TPU v7x, 128 devices: a whole 4x4x4 slice. The times are simulated.
128 devices in a mesh: gx: 8 (over z, core), gy: 16 (over y, x).
Axes of the slice: x: 4, y: 4, z: 4, core: 2. Of those that a mesh axis runs over, the one named last changes fastest.
Arguments:
- hidden_in: bfloat16 [32768, 3584], P(('gx', 'gy')), may hold values from -6 to 6
- lengths: int32 [8, 4], P('gx'), may hold values from 1 to 2048, 4096 in all within a row
- attn_norm: float32 [3584], replicated, may hold values from 0.5 to 1.5
- qkv_weight: bfloat16 [3584, 4608], P('gx', 'gy'), may hold values from -0.09375 to 0.09375
- qkv_bias: float32 [4608], replicated, may hold values from -5 to 5
Outputs:
- attn: bfloat16 [32768, 3584], P(('gx', 'gy'))
- kv_rows: bfloat16 [32768, 1024], P(('gx', 'gy'))
Inputs may be any that keep to these rules, and one draw needn't show every extreme that they name: Each row of lengths sums to 4096; the longest of each row is exactly 2048.
All inputs are finite; a program needn't handle non-finite values.
Results may differ from a plain program's by a relative error of at most 0.0035.
The roundings to bfloat16 on the way count: a program that leaves them out, or rounds other values in their place, can miss the bound.
Values may be sent and summed in bfloat16 or wider, within the bound.
No kernel may reach another device: no remote copies, remote signals or barrier semaphores. Data moves between devices by JAX's collectives and lax.ppermute only.
A program may use at most 128 MiB of HBM per device.

v0:
```python
import math
import jax
import jax.numpy as jnp
from jax import lax
from jax.sharding import PartitionSpec as P

HEADS = 28
KV_HEADS = 4
HEAD_DIM = 128
key_span = 512


def norm_rows(values, gain):
    wide = values.astype(jnp.float32)
    scale = lax.rsqrt(jnp.mean(wide * wide, axis=1, keepdims=True) + 1e-06)
    return (wide * scale * gain[None, :]).astype(jnp.bfloat16)


def segment_of(index, ends):
    return jnp.sum((ends[None, :] <= index[:, None]).astype(jnp.int32), axis=1)


def rotate(block, pos, heads):
    half = HEAD_DIM // 2
    freqs = 1000000.0 ** (-2.0 * jnp.arange(half, dtype=jnp.float32) / HEAD_DIM)
    angle = pos.astype(jnp.float32)[:, None, None] * freqs[None, None, :]
    wide = block.astype(jnp.float32).reshape(block.shape[0], heads, HEAD_DIM)
    first, second = (wide[..., :half], wide[..., half:])
    turned = jnp.concatenate(
        [
            first * jnp.cos(angle) - second * jnp.sin(angle),
            second * jnp.cos(angle) + first * jnp.sin(angle),
        ],
        axis=2,
    )
    return turned.reshape(block.shape[0], heads * HEAD_DIM).astype(jnp.bfloat16)


def project_joined(normed, weight, bias):
    grouped = lax.all_gather(normed, "gy", axis=0, tiled=True)
    summed = jnp.dot(
        grouped,
        lax.all_gather(weight, "gx", axis=0, tiled=True),
        preferred_element_type=jnp.float32,
    )
    width = weight.shape[1]
    bias_block = lax.dynamic_slice_in_dim(bias, lax.axis_index("gy") * width, width, 0)
    block_out = (summed + bias_block[None, :]).astype(jnp.bfloat16)
    return lax.all_to_all(block_out, "gy", split_axis=0, concat_axis=1, tiled=True)


def on_device(hidden_in, lengths, attn_norm, qkv_weight, qkv_bias):
    rows = hidden_in.shape[0]
    first = lax.axis_index("gy") * rows
    row_lengths = lengths[0]
    qdim = HEADS * HEAD_DIM
    kdim = KV_HEADS * HEAD_DIM
    group = HEADS // KV_HEADS
    normed = norm_rows(hidden_in, attn_norm)
    joined = project_joined(normed, qkv_weight, qkv_bias)
    ends = jnp.cumsum(row_lengths)
    tokens_here = first + jnp.arange(rows, dtype=jnp.int32)
    before = ends[None, :] <= tokens_here[:, None]
    seg_here = jnp.sum(before.astype(jnp.int32), axis=1)
    begin = jnp.sum(jnp.where(before, row_lengths[None, :], 0), axis=1)
    pos = tokens_here - begin
    queries = rotate(joined[:, :qdim], pos, HEADS).reshape(rows, KV_HEADS, group, HEAD_DIM)
    keys = rotate(joined[:, qdim : qdim + kdim], pos, KV_HEADS)
    kv_rows = jnp.concatenate([keys, joined[:, qdim + kdim :]], axis=1)
    scale = 1.0 / HEAD_DIM**0.5

    def attend(carry, piece, start):
        running, total, summed = carry
        key_count = piece.shape[0]
        key_index = start + jnp.arange(key_count, dtype=jnp.int32)
        key_seg = segment_of(key_index, ends)
        key_part = piece[:, :kdim].reshape(key_count, KV_HEADS, HEAD_DIM)
        value_part = piece[:, kdim:].reshape(key_count, KV_HEADS, HEAD_DIM)
        scores = (
            jnp.einsum("rgho,ngo->ghrn", queries, key_part, preferred_element_type=jnp.float32)
            * scale
        )
        allowed = (seg_here[:, None] == key_seg[None, :]) & (
            key_index[None, :] <= tokens_here[:, None]
        )
        newest = jnp.maximum(running, jnp.max(jnp.where(allowed, scores, -1e30), axis=3))
        shrink = jnp.exp(running - newest)
        weights = jnp.where(allowed, jnp.exp(scores - newest[..., None]), 0.0)
        total = total * shrink + jnp.sum(weights, axis=3)
        summed = summed * shrink[..., None] + jnp.einsum(
            "ghrn,ngo->ghro",
            weights.astype(jnp.bfloat16),
            value_part,
            preferred_element_type=jnp.float32,
        )
        return (newest, total, summed)

    def visit(carry, piece, start):
        return attend(carry, piece, start)

    start_state = (
        jnp.full((KV_HEADS, group, rows), -1e30, jnp.float32),
        jnp.zeros((KV_HEADS, group, rows), jnp.float32),
        jnp.zeros((KV_HEADS, group, rows, HEAD_DIM), jnp.float32),
    )
    piece = lax.all_gather(kv_rows, "gy", axis=0, tiled=True)
    length = piece.shape[0]
    span = math.gcd(length, key_span)
    stacked = piece.reshape(length // span, span, piece.shape[1])
    offsets = jnp.arange(length // span, dtype=jnp.int32) * span

    def advance(state, item):
        return (visit(state, item[0], item[1]), None)

    final_state, unused = lax.scan(advance, start_state, (stacked, offsets))
    running, total, summed = final_state
    attn = (
        jnp.transpose(summed / total[..., None], (2, 0, 1, 3))
        .reshape(rows, qdim)
        .astype(jnp.bfloat16)
    )
    return (attn, kv_rows)


def solution(mesh):
    placed = (P(("gx", "gy"), None), P("gx", None), P(), P("gx", "gy"), P())
    return jax.shard_map(
        on_device,
        mesh=mesh,
        in_specs=placed,
        out_specs=(P(("gx", "gy"), None), P(("gx", "gy"), None)),
        check_vma=False,
    )
```

profile of v0, /device:TPU:0, one launch (start us, length us, event | category | flops | bytes accessed | tf_op | source)
XLA Modules:
  0.0 595.3 jit_solution(592481126304964280)
XLA Ops:
  7.2 0.7 all-gather.9.cloned.1.call-update
  7.9 1.9 fusion.17
  9.9 3.2 fusion.19
  13.2 0.8 dynamic_slice.11
  13.9 24.0 %all-gather.9.cloned.1.call-done = bf16[8,448,288]{1,2,0:T(8,128)(2,1)} async-done(((bf16[1,448,288]{1,2,0:T(8,128)(2,1)}), bf16[8,448,288]{1,2,0:T(8,128)(2,1)}) %all-gather.9.cloned.1.call-update) | async-done | bytes 2064400 | tf_op jit(solution)/shard_map/all_gather | solution.py:43
  38.0 3.0 copy.34
  41.0 3.6 reshape.172
  44.5 172.0 %all-gather.5.cloned.1.call-done = bf16[4096,3584]{1,0:T(8,128)(2,1)} async-done(((bf16[256,3584]{1,0:T(8,128)(2,1)}), bf16[4096,3584]{1,0:T(8,128)(2,1)}) %all-gather.5.cloned.1.call-update) | async-done | bytes 29360144 | tf_op jit(solution)/shard_map/all_gather | solution.py:40
  216.6 14.7 %fusion.16 = bf16[4096,288]{0,1:T(8,128)(2,1)S(1)} fusion(bf16[4096,3584]{1,0:T(8,128)(2,1)} %all-gather.5.cloned.1.call-done, bf16[3584,288]{0,1:T(8,128)(2,1)} %reshape.172, f32[288]{0:T(512)S(1)} %dynamic_slice.11), kind=kOutput, calls=%fused_computation.25 | convolution fusion | flops 8458076160 | bytes 33784960 | tf_op jit(solution)/shard_map/dot_general | solution.py:41
  231.3 1.7 copy.53
  233.0 5.3 all-to-all-start
  239.1 34.4 %all-to-all-done = bf16[16,256,288]{1,2,0:T(8,128)(2,1)S(1)} async-done(((bf16[16,256,288]{1,2,0:T(8,128)(2,1)}), bf16[16,256,288]{1,2,0:T(8,128)(2,1)S(1)}, u32[]{:S(2)}, u32[]{:S(2)}) %all-to-all-start) | async-done | bytes 2359328 | tf_op jit(solution)/shard_map/all_to_all | solution.py:49
  273.6 0.9 pad_maximum_fusion.1
  274.6 1.3 slice.42
  275.9 1.0 copy.40
  276.9 1.9 convert.19
  279.5 1.4 pad_maximum_fusion
  280.8 3.0 copy.37
  283.8 65.9 %all-gather.7.cloned.1.call-done = bf16[4096,1024]{0,1:T(8,128)(2,1)} async-done(((bf16[256,1024]{0,1:T(8,128)(2,1)}), bf16[4096,1024]{0,1:T(8,128)(2,1)}) %all-gather.7.cloned.1.call-update) | async-done | bytes 8388624 | tf_op jit(solution)/shard_map/all_gather | solution.py:106
  349.7 7.5 %copy.52 = bf16[128,8,8,512]{3,2,0,1:T(8,128)(2,1)} copy(bf16[128,8,8,512]{3,2,1,0:T(8,128)(2,1)} %bitcast.86) | data formatting | bytes 16777216 | tf_op jit(solution)/shard_map/reshape | solution.py:109
  357.2 222.0 %while.15 = (s32[]{:T(128)}, f32[4,7,256]{2,1,0:T(8,128)S(1)}, f32[4,7,256]{2,1,0:T(8,128)S(1)}, f32[4,7,256,128]{3,2,1,0:T(8,128)}, s32[256]{0:T(256)S(1)}, /*i...) while((s32[]{:T(128)}, f32[4,7,256]{2,1,0:T(8,128)S(1)}, ...), condition=%wide.region_8.9_spmd.clone, body=%wide.region_4.8_spmd.clone.sunk | while | flops 1922606336 | bytes 88814816 | solution.py:115
  358.7 1.3 dynamic-slice_bitcast_fusion.2
  360.1 6.5 %fusion.43 = (f32[4,7,256]{2,1,0:T(8,128)S(1)}, f32[4,512,256,7]{2,1,3,0:T(8,128)}) fusion(pred[256,512]{0,1:T(8,128)(4,1)S(1)} %compare_and_fusion.2, bf16[512,4,128,1]{0,2,3,1:T(8,128)(2,1)S(1)} %bitcast.80, bf16[256,4,7,128]{3,0,2,1:T(8,128)(2,1)S(1)} %get-tuple-element.270), kind=kOutput, calls=%fused_computation.3.clone.1 | convolution fusion | flops 950526976 | bytes 17199104 | tf_op jit(solution)/shard_map/while/body/eval_jaxpr/rgho,ngo->ghrn/dot_general | solution.py:80
  366.6 8.3 %fusion.44 = f32[4,7,256]{2,1,0:T(8,128)S(1)} fusion(f32[4,512,256,7]{2,1,3,0:T(8,128)} %get-tuple-element.234, f32[4,7,256]{2,1,0:T(8,128)S(1)} %select_maximum_fusion.2, pred[256,512]{0,1:T(8,128)(4,1)S(1)} %compare_and_fusion.2), kind=kLoop, calls=%fused_computation.7.clone.1 | loop fusion | flops 14672896 | bytes 14868480 | tf_op jit(solution)/shard_map/while/body/eval_jaxpr/reduce_sum | solution.py:89
  375.0 8.0 %fusion.46 = f32[4,7,256,128]{3,2,1,0:T(8,128)S(1)} fusion(f32[4,7,256,128]{3,2,1,0:T(8,128)S(1)} %copy-done.1, bf16[512,4,128,1]{0,2,3,1:T(8,128)(2,1)S(1)} %bitcast.82, f32[4,512,256,7]{2,1,3,0:T(8,128)} %get-tuple-element.234, f32[4,7,256]{2,1,0:T(8,128)S(1)} %select_maximum_fusion.2, pred[256,512]{0,1:T(8,128)(4,1)S(1)} %compare_and_fusion.2, ...), kind=kOutput, calls=%fused_computation.11.clone.1 | convolution fusion | flops 956956672 | bytes 22732800 | tf_op jit(solution)/shard_map/while/body/eval_jaxpr/ghrn,ngo->ghro/dot_general | solution.py:90
  383.0 1.9 copy-done.2
  386.5 1.3 dynamic-slice_bitcast_fusion.2
  387.8 6.5 %fusion.43 = (f32[4,7,256]{2,1,0:T(8,128)S(1)}, f32[4,512,256,7]{2,1,3,0:T(8,128)}) fusion(pred[256,512]{0,1:T(8,128)(4,1)S(1)} %compare_and_fusion.2, bf16[512,4,128,1]{0,2,3,1:T(8,128)(2,1)S(1)} %bitcast.80, bf16[256,4,7,128]{3,0,2,1:T(8,128)(2,1)S(1)} %get-tuple-element.270), kind=kOutput, calls=%fused_computation.3.clone.1 | convolution fusion | flops 950526976 | bytes 17199104 | tf_op jit(solution)/shard_map/while/body/eval_jaxpr/rgho,ngo->ghrn/dot_general | solution.py:80
  394.4 8.3 %fusion.44 = f32[4,7,256]{2,1,0:T(8,128)S(1)} fusion(f32[4,512,256,7]{2,1,3,0:T(8,128)} %get-tuple-element.234, f32[4,7,256]{2,1,0:T(8,128)S(1)} %select_maximum_fusion.2, pred[256,512]{0,1:T(8,128)(4,1)S(1)} %compare_and_fusion.2), kind=kLoop, calls=%fused_computation.7.clone.1 | loop fusion | flops 14672896 | bytes 14868480 | tf_op jit(solution)/shard_map/while/body/eval_jaxpr/reduce_sum | solution.py:89
  402.7 8.0 %fusion.46 = f32[4,7,256,128]{3,2,1,0:T(8,128)S(1)} fusion(f32[4,7,256,128]{3,2,1,0:T(8,128)S(1)} %copy-done.1, bf16[512,4,128,1]{0,2,3,1:T(8,128)(2,1)S(1)} %bitcast.82, f32[4,512,256,7]{2,1,3,0:T(8,128)} %get-tuple-element.234, f32[4,7,256]{2,1,0:T(8,128)S(1)} %select_maximum_fusion.2, pred[256,512]{0,1:T(8,128)(4,1)S(1)} %compare_and_fusion.2, ...), kind=kOutput, calls=%fused_computation.11.clone.1 | convolution fusion | flops 956956672 | bytes 22732800 | tf_op jit(solution)/shard_map/while/body/eval_jaxpr/ghrn,ngo->ghro/dot_general | solution.py:90
  410.8 1.9 copy-done.2
  414.2 1.3 dynamic-slice_bitcast_fusion.2
  415.6 6.5 %fusion.43 = (f32[4,7,256]{2,1,0:T(8,128)S(1)}, f32[4,512,256,7]{2,1,3,0:T(8,128)}) fusion(pred[256,512]{0,1:T(8,128)(4,1)S(1)} %compare_and_fusion.2, bf16[512,4,128,1]{0,2,3,1:T(8,128)(2,1)S(1)} %bitcast.80, bf16[256,4,7,128]{3,0,2,1:T(8,128)(2,1)S(1)} %get-tuple-element.270), kind=kOutput, calls=%fused_computation.3.clone.1 | convolution fusion | flops 950526976 | bytes 17199104 | tf_op jit(solution)/shard_map/while/body/eval_jaxpr/rgho,ngo->ghrn/dot_general | solution.py:80
  422.1 8.3 %fusion.44 = f32[4,7,256]{2,1,0:T(8,128)S(1)} fusion(f32[4,512,256,7]{2,1,3,0:T(8,128)} %get-tuple-element.234, f32[4,7,256]{2,1,0:T(8,128)S(1)} %select_maximum_fusion.2, pred[256,512]{0,1:T(8,128)(4,1)S(1)} %compare_and_fusion.2), kind=kLoop, calls=%fused_computation.7.clone.1 | loop fusion | flops 14672896 | bytes 14868480 | tf_op jit(solution)/shard_map/while/body/eval_jaxpr/reduce_sum | solution.py:89
  430.5 8.0 %fusion.46 = f32[4,7,256,128]{3,2,1,0:T(8,128)S(1)} fusion(f32[4,7,256,128]{3,2,1,0:T(8,128)S(1)} %copy-done.1, bf16[512,4,128,1]{0,2,3,1:T(8,128)(2,1)S(1)} %bitcast.82, f32[4,512,256,7]{2,1,3,0:T(8,128)} %get-tuple-element.234, f32[4,7,256]{2,1,0:T(8,128)S(1)} %select_maximum_fusion.2, pred[256,512]{0,1:T(8,128)(4,1)S(1)} %compare_and_fusion.2, ...), kind=kOutput, calls=%fused_computation.11.clone.1 | convolution fusion | flops 956956672 | bytes 22732800 | tf_op jit(solution)/shard_map/while/body/eval_jaxpr/ghrn,ngo->ghro/dot_general | solution.py:90
  438.5 1.9 copy-done.2
  441.9 1.3 dynamic-slice_bitcast_fusion.2
  443.3 6.5 %fusion.43 = (f32[4,7,256]{2,1,0:T(8,128)S(1)}, f32[4,512,256,7]{2,1,3,0:T(8,128)}) fusion(pred[256,512]{0,1:T(8,128)(4,1)S(1)} %compare_and_fusion.2, bf16[512,4,128,1]{0,2,3,1:T(8,128)(2,1)S(1)} %bitcast.80, bf16[256,4,7,128]{3,0,2,1:T(8,128)(2,1)S(1)} %get-tuple-element.270), kind=kOutput, calls=%fused_computation.3.clone.1 | convolution fusion | flops 950526976 | bytes 17199104 | tf_op jit(solution)/shard_map/while/body/eval_jaxpr/rgho,ngo->ghrn/dot_general | solution.py:80
  449.9 8.3 %fusion.44 = f32[4,7,256]{2,1,0:T(8,128)S(1)} fusion(f32[4,512,256,7]{2,1,3,0:T(8,128)} %get-tuple-element.234, f32[4,7,256]{2,1,0:T(8,128)S(1)} %select_maximum_fusion.2, pred[256,512]{0,1:T(8,128)(4,1)S(1)} %compare_and_fusion.2), kind=kLoop, calls=%fused_computation.7.clone.1 | loop fusion | flops 14672896 | bytes 14868480 | tf_op jit(solution)/shard_map/while/body/eval_jaxpr/reduce_sum | solution.py:89
  458.2 8.0 %fusion.46 = f32[4,7,256,128]{3,2,1,0:T(8,128)S(1)} fusion(f32[4,7,256,128]{3,2,1,0:T(8,128)S(1)} %copy-done.1, bf16[512,4,128,1]{0,2,3,1:T(8,128)(2,1)S(1)} %bitcast.82, f32[4,512,256,7]{2,1,3,0:T(8,128)} %get-tuple-element.234, f32[4,7,256]{2,1,0:T(8,128)S(1)} %select_maximum_fusion.2, pred[256,512]{0,1:T(8,128)(4,1)S(1)} %compare_and_fusion.2, ...), kind=kOutput, calls=%fused_computation.11.clone.1 | convolution fusion | flops 956956672 | bytes 22732800 | tf_op jit(solution)/shard_map/while/body/eval_jaxpr/ghrn,ngo->ghro/dot_general | solution.py:90
  466.3 1.9 copy-done.2
  469.7 1.3 dynamic-slice_bitcast_fusion.2
  471.1 6.5 %fusion.43 = (f32[4,7,256]{2,1,0:T(8,128)S(1)}, f32[4,512,256,7]{2,1,3,0:T(8,128)}) fusion(pred[256,512]{0,1:T(8,128)(4,1)S(1)} %compare_and_fusion.2, bf16[512,4,128,1]{0,2,3,1:T(8,128)(2,1)S(1)} %bitcast.80, bf16[256,4,7,128]{3,0,2,1:T(8,128)(2,1)S(1)} %get-tuple-element.270), kind=kOutput, calls=%fused_computation.3.clone.1 | convolution fusion | flops 950526976 | bytes 17199104 | tf_op jit(solution)/shard_map/while/body/eval_jaxpr/rgho,ngo->ghrn/dot_general | solution.py:80
  477.6 8.3 %fusion.44 = f32[4,7,256]{2,1,0:T(8,128)S(1)} fusion(f32[4,512,256,7]{2,1,3,0:T(8,128)} %get-tuple-element.234, f32[4,7,256]{2,1,0:T(8,128)S(1)} %select_maximum_fusion.2, pred[256,512]{0,1:T(8,128)(4,1)S(1)} %compare_and_fusion.2), kind=kLoop, calls=%fused_computation.7.clone.1 | loop fusion | flops 14672896 | bytes 14868480 | tf_op jit(solution)/shard_map/while/body/eval_jaxpr/reduce_sum | solution.py:89
  486.0 8.0 %fusion.46 = f32[4,7,256,128]{3,2,1,0:T(8,128)S(1)} fusion(f32[4,7,256,128]{3,2,1,0:T(8,128)S(1)} %copy-done.1, bf16[512,4,128,1]{0,2,3,1:T(8,128)(2,1)S(1)} %bitcast.82, f32[4,512,256,7]{2,1,3,0:T(8,128)} %get-tuple-element.234, f32[4,7,256]{2,1,0:T(8,128)S(1)} %select_maximum_fusion.2, pred[256,512]{0,1:T(8,128)(4,1)S(1)} %compare_and_fusion.2, ...), kind=kOutput, calls=%fused_computation.11.clone.1 | convolution fusion | flops 956956672 | bytes 22732800 | tf_op jit(solution)/shard_map/while/body/eval_jaxpr/ghrn,ngo->ghro/dot_general | solution.py:90
  494.0 1.9 copy-done.2
  497.4 1.3 dynamic-slice_bitcast_fusion.2
  498.8 6.5 %fusion.43 = (f32[4,7,256]{2,1,0:T(8,128)S(1)}, f32[4,512,256,7]{2,1,3,0:T(8,128)}) fusion(pred[256,512]{0,1:T(8,128)(4,1)S(1)} %compare_and_fusion.2, bf16[512,4,128,1]{0,2,3,1:T(8,128)(2,1)S(1)} %bitcast.80, bf16[256,4,7,128]{3,0,2,1:T(8,128)(2,1)S(1)} %get-tuple-element.270), kind=kOutput, calls=%fused_computation.3.clone.1 | convolution fusion | flops 950526976 | bytes 17199104 | tf_op jit(solution)/shard_map/while/body/eval_jaxpr/rgho,ngo->ghrn/dot_general | solution.py:80
  505.4 8.3 %fusion.44 = f32[4,7,256]{2,1,0:T(8,128)S(1)} fusion(f32[4,512,256,7]{2,1,3,0:T(8,128)} %get-tuple-element.234, f32[4,7,256]{2,1,0:T(8,128)S(1)} %select_maximum_fusion.2, pred[256,512]{0,1:T(8,128)(4,1)S(1)} %compare_and_fusion.2), kind=kLoop, calls=%fused_computation.7.clone.1 | loop fusion | flops 14672896 | bytes 14868480 | tf_op jit(solution)/shard_map/while/body/eval_jaxpr/reduce_sum | solution.py:89
  513.7 8.0 %fusion.46 = f32[4,7,256,128]{3,2,1,0:T(8,128)S(1)} fusion(f32[4,7,256,128]{3,2,1,0:T(8,128)S(1)} %copy-done.1, bf16[512,4,128,1]{0,2,3,1:T(8,128)(2,1)S(1)} %bitcast.82, f32[4,512,256,7]{2,1,3,0:T(8,128)} %get-tuple-element.234, f32[4,7,256]{2,1,0:T(8,128)S(1)} %select_maximum_fusion.2, pred[256,512]{0,1:T(8,128)(4,1)S(1)} %compare_and_fusion.2, ...), kind=kOutput, calls=%fused_computation.11.clone.1 | convolution fusion | flops 956956672 | bytes 22732800 | tf_op jit(solution)/shard_map/while/body/eval_jaxpr/ghrn,ngo->ghro/dot_general | solution.py:90
  521.8 1.9 copy-done.2
  525.2 1.3 dynamic-slice_bitcast_fusion.2
  526.6 6.5 %fusion.43 = (f32[4,7,256]{2,1,0:T(8,128)S(1)}, f32[4,512,256,7]{2,1,3,0:T(8,128)}) fusion(pred[256,512]{0,1:T(8,128)(4,1)S(1)} %compare_and_fusion.2, bf16[512,4,128,1]{0,2,3,1:T(8,128)(2,1)S(1)} %bitcast.80, bf16[256,4,7,128]{3,0,2,1:T(8,128)(2,1)S(1)} %get-tuple-element.270), kind=kOutput, calls=%fused_computation.3.clone.1 | convolution fusion | flops 950526976 | bytes 17199104 | tf_op jit(solution)/shard_map/while/body/eval_jaxpr/rgho,ngo->ghrn/dot_general | solution.py:80
  533.1 8.3 %fusion.44 = f32[4,7,256]{2,1,0:T(8,128)S(1)} fusion(f32[4,512,256,7]{2,1,3,0:T(8,128)} %get-tuple-element.234, f32[4,7,256]{2,1,0:T(8,128)S(1)} %select_maximum_fusion.2, pred[256,512]{0,1:T(8,128)(4,1)S(1)} %compare_and_fusion.2), kind=kLoop, calls=%fused_computation.7.clone.1 | loop fusion | flops 14672896 | bytes 14868480 | tf_op jit(solution)/shard_map/while/body/eval_jaxpr/reduce_sum | solution.py:89
  541.5 8.0 %fusion.46 = f32[4,7,256,128]{3,2,1,0:T(8,128)S(1)} fusion(f32[4,7,256,128]{3,2,1,0:T(8,128)S(1)} %copy-done.1, bf16[512,4,128,1]{0,2,3,1:T(8,128)(2,1)S(1)} %bitcast.82, f32[4,512,256,7]{2,1,3,0:T(8,128)} %get-tuple-element.234, f32[4,7,256]{2,1,0:T(8,128)S(1)} %select_maximum_fusion.2, pred[256,512]{0,1:T(8,128)(4,1)S(1)} %compare_and_fusion.2, ...), kind=kOutput, calls=%fused_computation.11.clone.1 | convolution fusion | flops 956956672 | bytes 22732800 | tf_op jit(solution)/shard_map/while/body/eval_jaxpr/ghrn,ngo->ghro/dot_general | solution.py:90
  549.5 1.9 copy-done.2
  552.9 1.3 dynamic-slice_bitcast_fusion.2
  554.3 6.5 %fusion.43 = (f32[4,7,256]{2,1,0:T(8,128)S(1)}, f32[4,512,256,7]{2,1,3,0:T(8,128)}) fusion(pred[256,512]{0,1:T(8,128)(4,1)S(1)} %compare_and_fusion.2, bf16[512,4,128,1]{0,2,3,1:T(8,128)(2,1)S(1)} %bitcast.80, bf16[256,4,7,128]{3,0,2,1:T(8,128)(2,1)S(1)} %get-tuple-element.270), kind=kOutput, calls=%fused_computation.3.clone.1 | convolution fusion | flops 950526976 | bytes 17199104 | tf_op jit(solution)/shard_map/while/body/eval_jaxpr/rgho,ngo->ghrn/dot_general | solution.py:80
  560.9 8.3 %fusion.44 = f32[4,7,256]{2,1,0:T(8,128)S(1)} fusion(f32[4,512,256,7]{2,1,3,0:T(8,128)} %get-tuple-element.234, f32[4,7,256]{2,1,0:T(8,128)S(1)} %select_maximum_fusion.2, pred[256,512]{0,1:T(8,128)(4,1)S(1)} %compare_and_fusion.2), kind=kLoop, calls=%fused_computation.7.clone.1 | loop fusion | flops 14672896 | bytes 14868480 | tf_op jit(solution)/shard_map/while/body/eval_jaxpr/reduce_sum | solution.py:89
  569.2 8.0 %fusion.46 = f32[4,7,256,128]{3,2,1,0:T(8,128)S(1)} fusion(f32[4,7,256,128]{3,2,1,0:T(8,128)S(1)} %copy-done.1, bf16[512,4,128,1]{0,2,3,1:T(8,128)(2,1)S(1)} %bitcast.82, f32[4,512,256,7]{2,1,3,0:T(8,128)} %get-tuple-element.234, f32[4,7,256]{2,1,0:T(8,128)S(1)} %select_maximum_fusion.2, pred[256,512]{0,1:T(8,128)(4,1)S(1)} %compare_and_fusion.2, ...), kind=kOutput, calls=%fused_computation.11.clone.1 | convolution fusion | flops 956956672 | bytes 22732800 | tf_op jit(solution)/shard_map/while/body/eval_jaxpr/ghrn,ngo->ghro/dot_general | solution.py:90
  577.3 1.9 copy-done.2
  579.1 4.6 copy.38
  583.7 2.5 divide_convert_fusion
  586.2 2.6 copy.39
  (121 shorter events, 14.8 us)
Async XLA Ops:
  7.2 30.8 %all-gather.9.cloned.1.call-start = ((), (), s32[]{:S(2)}) async-start(), calls=%async_computation.3 | async-start | bytes 2654208 | tf_op jit(solution)/shard_map/all_gather | solution.py:43
  7.9 208.7 %all-gather.5.cloned.1.call-start = ((), (), s32[]{:S(2)}) async-start(), calls=%async_computation.1 | async-start | bytes 31195136 | tf_op jit(solution)/shard_map/all_gather | solution.py:40
  231.3 7.2 %copy-start.3 = (s32[1,4]{1,0:T(1,128)S(1)}, s32[1,4]{1,0:T(1,128)}, u32[]{:S(2)}) copy-start(s32[1,4]{1,0:T(1,128)} %param.8) | copy-start | bytes 52
  233.0 40.5 %all-to-all-start = ((bf16[16,256,288]{1,2,0:T(8,128)(2,1)}), bf16[16,256,288]{1,2,0:T(8,128)(2,1)S(1)}, u32[]{:S(2)}, u32[]{:S(2)}) async-start(bf16[16,256,288]{1,2,0:T(8,128)(2,1)} %bitcast.85), calls=%async_computation | async-start | bytes 4718592 | tf_op jit(solution)/shard_map/all_to_all | solution.py:49
  238.2 111.5 %all-gather.7.cloned.1.call-start = ((), (), s32[]{:S(2)}) async-start(), calls=%async_computation.2 | async-start | bytes 8912896 | tf_op jit(solution)/shard_map/all_gather | solution.py:106
  274.5 1.4 copy-start
  366.6 8.4 %copy-start.1 = (f32[4,7,256,128]{3,2,1,0:T(8,128)S(1)}, f32[4,7,256,128]{3,2,1,0:T(8,128)}, u32[]{:S(2)}) copy-start(f32[4,7,256,128]{3,2,1,0:T(8,128)} %get-tuple-element.253) | copy-start | bytes 11010052 | tf_op jit(solution)/shard_map/while
  383.0 1.9 copy-start.2
  394.4 8.4 %copy-start.1 = (f32[4,7,256,128]{3,2,1,0:T(8,128)S(1)}, f32[4,7,256,128]{3,2,1,0:T(8,128)}, u32[]{:S(2)}) copy-start(f32[4,7,256,128]{3,2,1,0:T(8,128)} %get-tuple-element.253) | copy-start | bytes 11010052 | tf_op jit(solution)/shard_map/while
  410.8 1.9 copy-start.2
  422.1 8.4 %copy-start.1 = (f32[4,7,256,128]{3,2,1,0:T(8,128)S(1)}, f32[4,7,256,128]{3,2,1,0:T(8,128)}, u32[]{:S(2)}) copy-start(f32[4,7,256,128]{3,2,1,0:T(8,128)} %get-tuple-element.253) | copy-start | bytes 11010052 | tf_op jit(solution)/shard_map/while
  438.5 1.9 copy-start.2
  449.9 8.4 %copy-start.1 = (f32[4,7,256,128]{3,2,1,0:T(8,128)S(1)}, f32[4,7,256,128]{3,2,1,0:T(8,128)}, u32[]{:S(2)}) copy-start(f32[4,7,256,128]{3,2,1,0:T(8,128)} %get-tuple-element.253) | copy-start | bytes 11010052 | tf_op jit(solution)/shard_map/while
  466.3 1.9 copy-start.2
  477.6 8.4 %copy-start.1 = (f32[4,7,256,128]{3,2,1,0:T(8,128)S(1)}, f32[4,7,256,128]{3,2,1,0:T(8,128)}, u32[]{:S(2)}) copy-start(f32[4,7,256,128]{3,2,1,0:T(8,128)} %get-tuple-element.253) | copy-start | bytes 11010052 | tf_op jit(solution)/shard_map/while
  494.0 1.9 copy-start.2
  505.4 8.4 %copy-start.1 = (f32[4,7,256,128]{3,2,1,0:T(8,128)S(1)}, f32[4,7,256,128]{3,2,1,0:T(8,128)}, u32[]{:S(2)}) copy-start(f32[4,7,256,128]{3,2,1,0:T(8,128)} %get-tuple-element.253) | copy-start | bytes 11010052 | tf_op jit(solution)/shard_map/while
  521.8 1.9 copy-start.2
  533.1 8.4 %copy-start.1 = (f32[4,7,256,128]{3,2,1,0:T(8,128)S(1)}, f32[4,7,256,128]{3,2,1,0:T(8,128)}, u32[]{:S(2)}) copy-start(f32[4,7,256,128]{3,2,1,0:T(8,128)} %get-tuple-element.253) | copy-start | bytes 11010052 | tf_op jit(solution)/shard_map/while
  549.5 1.9 copy-start.2
  560.9 8.4 %copy-start.1 = (f32[4,7,256,128]{3,2,1,0:T(8,128)S(1)}, f32[4,7,256,128]{3,2,1,0:T(8,128)}, u32[]{:S(2)}) copy-start(f32[4,7,256,128]{3,2,1,0:T(8,128)} %get-tuple-element.253) | copy-start | bytes 11010052 | tf_op jit(solution)/shard_map/while
  577.3 1.9 copy-start.2
Sparse Core Ops, SparseCore 0:
  9.7 28.2 all-gather.8
  40.7 175.8 all-gather.4
  274.6 75.0 all-gather.6
where the time goes:
time: 597 us; the launch traced here: 595 us
  waiting for transfers between devices  297 us (50%)
  matrix products  131 us (22%)
  other arithmetic  87.5 us (15%)
  local copies, waits for them, and re-layouts  59.6 us (10%)
  between operations  13.9 us (2%)
    all_gather x1, waiting for transfers between devices, project_joined(): grouped = lax.all_gather(normed, 'gy', axis=0, tiled=True)  172 us
    reduce_sum x8, other arithmetic, attend(): total = total * shrink + jnp.sum(weights, axis=3)  66.5 us
    all_gather x1, waiting for transfers between devices, on_device(): piece = lax.all_gather(kv_rows, 'gy', axis=0, tiled=True)  65.9 us
    dot_general x8, matrix products, attend(): jnp.einsum('ghrn,ngo->ghro', weights.astype(jnp.bfloat16), value_part, pr...  64.3 us
    dot_general x8, matrix products, attend(): jnp.einsum('rgho,ngo->ghrn', queries, key_part, preferred_element_type=jn...  52.3 us
    all_to_all x1, waiting for transfers between devices, project_joined(): lax.all_to_all(block_out, 'gy', split_axis=0, concat_axis=1, tiled=True)  34.4 us
    all_gather x1, waiting for transfers between devices, project_joined(): lax.all_gather(weight, 'gx', axis=0, tiled=True)  24 us
    while x40, local copies, waits for them, and re-layouts  15 us
  transfers between devices with their start and end apart: 4, of which 4 were waited for; matrix products, arithmetic and copies ran while one was open for 4% of the time, Pallas kernels for 0%

commit v1 on v0

--- a/solution.py
+++ b/solution.py
@@ -46,7 +46,10 @@
     width = weight.shape[1]
     bias_block = lax.dynamic_slice_in_dim(bias, lax.axis_index("gy") * width, width, 0)
     block_out = (summed + bias_block[None, :]).astype(jnp.bfloat16)
-    return lax.all_to_all(block_out, "gy", split_axis=0, concat_axis=1, tiled=True)
+    define_yards_on = lambda chunk: jnp.concatenate(
+        lax.all_to_all(jnp.stack(jnp.split(chunk, lax.axis_size("gy"), axis=0)), "gy", 0, 0), axis=1
+    )
+    return define_yards_on(block_out)
 
 
 def on_device(hidden_in, lengths, attn_norm, qkv_weight, qkv_bias):

time: 597 us -> 613 us (1.027)
  local copies, waits for them, and re-layouts: 59.6 us -> 83.3 us
  waiting for transfers between devices: 297 us -> 286 us
    unnamed x8 -> x29, local copies, waits for them, and re-layouts: 10.1 us -> 24.9 us
    dynamic_slice x8 -> x24, local copies, waits for them, and re-layouts: 4.66 us -> 19.4 us  [on_device(): final_state, unused = lax.scan(advance, start_state, (stacked, offsets))]
    all_gather x1, waiting for transfers between devices: 65.9 us -> 54.2 us  [on_device(): piece = lax.all_gather(kv_rows, 'gy', axis=0, tiled=True)]
    while x40 -> x56, local copies, waits for them, and re-layouts: 15 us -> 26.2 us
    squeeze x8 -> x0, local copies, waits for them, and re-layouts: 10.4 us -> none  [on_device(): final_state, unused = lax.scan(advance, start_state, (stacked, offsets))]
    reshape x1 -> x0, local copies, waits for them, and re-layouts: 7.45 us -> none  [on_device(): stacked = piece.reshape(length // span, span, piece.shape[1])]
  transfers between devices with their start and end apart: 4 -> 4, of which waited for: 4 -> 4; matrix products, arithmetic and copies ran while one was open for 4% -> 5% of each run, Pallas kernels for 0% -> 0%
where the time goes in v1:
time: 613 us; the launch traced here: 611 us
  waiting for transfers between devices  286 us (47%)
  matrix products  131 us (21%)
  other arithmetic  91 us (15%)
  local copies, waits for them, and re-layouts  83.3 us (14%)
  between operations  13.9 us (2%)
    all_gather x1, waiting for transfers between devices, project_joined(): grouped = lax.all_gather(normed, 'gy', axis=0, tiled=True)  172 us
    reduce_sum x8, other arithmetic, attend(): total = total * shrink + jnp.sum(weights, axis=3)  66.5 us
    dot_general x8, matrix products, attend(): jnp.einsum('ghrn,ngo->ghro', weights.astype(jnp.bfloat16), value_part, pr...  64.3 us
    all_gather x1, waiting for transfers between devices, on_device(): piece = lax.all_gather(kv_rows, 'gy', axis=0, tiled=True)  54.2 us
    dot_general x8, matrix products, attend(): jnp.einsum('rgho,ngo->ghrn', queries, key_part, preferred_element_type=jn...  52.1 us
    all_to_all x1, waiting for transfers between devices, project_joined(): lax.all_to_all(jnp.stack(jnp.split(chunk, lax.axis_size('gy'), axis=0)),...  33.7 us
    while x56, local copies, waits for them, and re-layouts  26.2 us
    unnamed x29, local copies, waits for them, and re-layouts  24.9 us
  transfers between devices with their start and end apart: 4, of which 4 were waited for; matrix products, arithmetic and copies ran while one was open for 5% of the time, Pallas kernels for 0%

profile of v1, /device:TPU:0, one launch (start us, length us, event | category | flops | bytes accessed | tf_op | source)
XLA Modules:
  0.0 610.9 jit_solution(10762567063647683288)
XLA Ops:
  8.0 1.9 fusion.17
  9.9 2.5 fusion.19
  13.2 24.8 %all-gather.9.cloned.1.call-done = bf16[8,448,288]{1,2,0:T(8,128)(2,1)} async-done(((bf16[1,448,288]{1,2,0:T(8,128)(2,1)}), bf16[8,448,288]{1,2,0:T(8,128)(2,1)}) %all-gather.9.cloned.1.call-update) | async-done | bytes 2064400 | tf_op jit(solution)/shard_map/all_gather | solution.py:43
  38.0 3.0 copy.41
  41.0 3.6 reshape.177
  44.5 172.1 %all-gather.5.cloned.1.call-done = bf16[4096,3584]{1,0:T(8,128)(2,1)} async-done(((bf16[256,3584]{1,0:T(8,128)(2,1)}), bf16[4096,3584]{1,0:T(8,128)(2,1)}) %all-gather.5.cloned.1.call-update) | async-done | bytes 29360144 | tf_op jit(solution)/shard_map/all_gather | solution.py:40
  216.6 14.7 %fusion.16 = bf16[4096,288]{0,1:T(8,128)(2,1)S(1)} fusion(bf16[4096,3584]{1,0:T(8,128)(2,1)} %all-gather.5.cloned.1.call-done, bf16[3584,288]{0,1:T(8,128)(2,1)} %reshape.177, f32[288]{0:T(512)S(1)} %dynamic_slice.11), kind=kOutput, calls=%fused_computation.24 | convolution fusion | flops 8458076160 | bytes 33784960 | tf_op jit(solution)/shard_map/dot_general | solution.py:41
  242.1 5.4 all-to-all-start
  249.1 33.7 %all-to-all-done = bf16[16,256,288]{1,2,0:T(8,128)(2,1)S(1)} async-done(((bf16[16,256,288]{1,2,0:T(8,128)(2,1)}), bf16[16,256,288]{1,2,0:T(8,128)(2,1)S(1)}, u32[]{:S(2)}, u32[]{:S(2)}) %all-to-all-start) | async-done | bytes 2359328 | tf_op jit(solution)/shard_map/all_to_all | solution.py:50
  289.4 1.7 fusion.40
  291.1 3.6 copy.61
  294.6 2.5 copy.62
  297.1 4.4 subtract_convert_fusion
  301.6 2.2 pad_maximum_fusion
  303.8 54.2 %all-gather.7.cloned.1.call-done = bf16[4096,1024]{1,0:T(8,128)(2,1)} async-done(((bf16[256,1024]{1,0:T(8,128)(2,1)}), bf16[4096,1024]{1,0:T(8,128)(2,1)}) %all-gather.7.cloned.1.call-update) | async-done | bytes 8388624 | tf_op jit(solution)/shard_map/all_gather | solution.py:109
  358.1 236.7 %while.15 = (s32[]{:T(128)}, f32[4,7,256]{2,1,0:T(8,128)S(1)}, f32[4,7,256]{2,1,0:T(8,128)S(1)}, f32[4,7,256,128]{3,2,1,0:T(8,128)}, s32[256]{0:T(256)S(1)}, /*i...) while((s32[]{:T(128)}, f32[4,7,256]{2,1,0:T(8,128)S(1)}, ...), condition=%wide.region_8.9_spmd.clone, body=%wide.region_4.8_spmd.clone.sunk | while | flops 1922606336 | bytes 98252016 | solution.py:118
  359.5 1.3 constant_dynamic-slice_fusion.2
  361.4 1.4 copy-done
  362.9 6.5 %fusion.61 = (f32[4,7,256]{2,1,0:T(8,128)S(1)}, f32[4,512,256,7]{2,1,3,0:T(8,128)}) fusion(pred[256,512]{0,1:T(8,128)(4,1)S(1)} %compare_and_fusion.2, bf16[512,4,128,1]{0,2,3,1:T(8,128)(2,1)S(1)} %bitcast.141, bf16[256,4,7,128]{3,0,2,1:T(8,128)(2,1)S(1)} %copy-done), kind=kOutput, calls=%fused_computation.3.clone.1 | convolution fusion | flops 950526976 | bytes 17199104 | tf_op jit(solution)/shard_map/while/body/eval_jaxpr/rgho,ngo->ghrn/dot_general | solution.py:83
  369.4 8.3 %fusion.62 = f32[4,7,256]{2,1,0:T(8,128)S(1)} fusion(f32[4,512,256,7]{2,1,3,0:T(8,128)} %get-tuple-element.238, f32[4,7,256]{2,1,0:T(8,128)S(1)} %select_maximum_fusion.2, pred[256,512]{0,1:T(8,128)(4,1)S(1)} %compare_and_fusion.2), kind=kLoop, calls=%fused_computation.7.clone.1 | loop fusion | flops 14672896 | bytes 14868480 | tf_op jit(solution)/shard_map/while/body/eval_jaxpr/reduce_sum | solution.py:92
  377.7 8.0 %fusion.64 = f32[4,7,256,128]{3,2,1,0:T(8,128)S(1)} fusion(f32[4,7,256,128]{3,2,1,0:T(8,128)S(1)} %copy-done.2, bf16[512,4,128,1]{0,2,3,1:T(8,128)(2,1)S(1)} %bitcast.143, f32[4,512,256,7]{2,1,3,0:T(8,128)} %get-tuple-element.238, f32[4,7,256]{2,1,0:T(8,128)S(1)} %select_maximum_fusion.2, pred[256,512]{0,1:T(8,128)(4,1)S(1)} %compare_and_fusion.2, ...), kind=kOutput, calls=%fused_computation.11.clone.1 | convolution fusion | flops 956956672 | bytes 22732800 | tf_op jit(solution)/shard_map/while/body/eval_jaxpr/ghrn,ngo->ghro/dot_general | solution.py:93
  385.8 1.9 copy-done.3
  389.1 1.3 constant_dynamic-slice_fusion.2
  391.0 1.4 copy-done
  392.4 6.5 %fusion.61 = (f32[4,7,256]{2,1,0:T(8,128)S(1)}, f32[4,512,256,7]{2,1,3,0:T(8,128)}) fusion(pred[256,512]{0,1:T(8,128)(4,1)S(1)} %compare_and_fusion.2, bf16[512,4,128,1]{0,2,3,1:T(8,128)(2,1)S(1)} %bitcast.141, bf16[256,4,7,128]{3,0,2,1:T(8,128)(2,1)S(1)} %copy-done), kind=kOutput, calls=%fused_computation.3.clone.1 | convolution fusion | flops 950526976 | bytes 17199104 | tf_op jit(solution)/shard_map/while/body/eval_jaxpr/rgho,ngo->ghrn/dot_general | solution.py:83
  399.0 8.3 %fusion.62 = f32[4,7,256]{2,1,0:T(8,128)S(1)} fusion(f32[4,512,256,7]{2,1,3,0:T(8,128)} %get-tuple-element.238, f32[4,7,256]{2,1,0:T(8,128)S(1)} %select_maximum_fusion.2, pred[256,512]{0,1:T(8,128)(4,1)S(1)} %compare_and_fusion.2), kind=kLoop, calls=%fused_computation.7.clone.1 | loop fusion | flops 14672896 | bytes 14868480 | tf_op jit(solution)/shard_map/while/body/eval_jaxpr/reduce_sum | solution.py:92
  407.3 8.0 %fusion.64 = f32[4,7,256,128]{3,2,1,0:T(8,128)S(1)} fusion(f32[4,7,256,128]{3,2,1,0:T(8,128)S(1)} %copy-done.2, bf16[512,4,128,1]{0,2,3,1:T(8,128)(2,1)S(1)} %bitcast.143, f32[4,512,256,7]{2,1,3,0:T(8,128)} %get-tuple-element.238, f32[4,7,256]{2,1,0:T(8,128)S(1)} %select_maximum_fusion.2, pred[256,512]{0,1:T(8,128)(4,1)S(1)} %compare_and_fusion.2, ...), kind=kOutput, calls=%fused_computation.11.clone.1 | convolution fusion | flops 956956672 | bytes 22732800 | tf_op jit(solution)/shard_map/while/body/eval_jaxpr/ghrn,ngo->ghro/dot_general | solution.py:93
  415.4 1.9 copy-done.3
  418.7 1.3 constant_dynamic-slice_fusion.2
  420.6 1.4 copy-done
  422.0 6.5 %fusion.61 = (f32[4,7,256]{2,1,0:T(8,128)S(1)}, f32[4,512,256,7]{2,1,3,0:T(8,128)}) fusion(pred[256,512]{0,1:T(8,128)(4,1)S(1)} %compare_and_fusion.2, bf16[512,4,128,1]{0,2,3,1:T(8,128)(2,1)S(1)} %bitcast.141, bf16[256,4,7,128]{3,0,2,1:T(8,128)(2,1)S(1)} %copy-done), kind=kOutput, calls=%fused_computation.3.clone.1 | convolution fusion | flops 950526976 | bytes 17199104 | tf_op jit(solution)/shard_map/while/body/eval_jaxpr/rgho,ngo->ghrn/dot_general | solution.py:83
  428.5 8.3 %fusion.62 = f32[4,7,256]{2,1,0:T(8,128)S(1)} fusion(f32[4,512,256,7]{2,1,3,0:T(8,128)} %get-tuple-element.238, f32[4,7,256]{2,1,0:T(8,128)S(1)} %select_maximum_fusion.2, pred[256,512]{0,1:T(8,128)(4,1)S(1)} %compare_and_fusion.2), kind=kLoop, calls=%fused_computation.7.clone.1 | loop fusion | flops 14672896 | bytes 14868480 | tf_op jit(solution)/shard_map/while/body/eval_jaxpr/reduce_sum | solution.py:92
  436.9 8.0 %fusion.64 = f32[4,7,256,128]{3,2,1,0:T(8,128)S(1)} fusion(f32[4,7,256,128]{3,2,1,0:T(8,128)S(1)} %copy-done.2, bf16[512,4,128,1]{0,2,3,1:T(8,128)(2,1)S(1)} %bitcast.143, f32[4,512,256,7]{2,1,3,0:T(8,128)} %get-tuple-element.238, f32[4,7,256]{2,1,0:T(8,128)S(1)} %select_maximum_fusion.2, pred[256,512]{0,1:T(8,128)(4,1)S(1)} %compare_and_fusion.2, ...), kind=kOutput, calls=%fused_computation.11.clone.1 | convolution fusion | flops 956956672 | bytes 22732800 | tf_op jit(solution)/shard_map/while/body/eval_jaxpr/ghrn,ngo->ghro/dot_general | solution.py:93
  444.9 1.9 copy-done.3
  448.2 1.3 constant_dynamic-slice_fusion.2
  450.2 1.4 copy-done
  451.6 6.5 %fusion.61 = (f32[4,7,256]{2,1,0:T(8,128)S(1)}, f32[4,512,256,7]{2,1,3,0:T(8,128)}) fusion(pred[256,512]{0,1:T(8,128)(4,1)S(1)} %compare_and_fusion.2, bf16[512,4,128,1]{0,2,3,1:T(8,128)(2,1)S(1)} %bitcast.141, bf16[256,4,7,128]{3,0,2,1:T(8,128)(2,1)S(1)} %copy-done), kind=kOutput, calls=%fused_computation.3.clone.1 | convolution fusion | flops 950526976 | bytes 17199104 | tf_op jit(solution)/shard_map/while/body/eval_jaxpr/rgho,ngo->ghrn/dot_general | solution.py:83
  458.1 8.3 %fusion.62 = f32[4,7,256]{2,1,0:T(8,128)S(1)} fusion(f32[4,512,256,7]{2,1,3,0:T(8,128)} %get-tuple-element.238, f32[4,7,256]{2,1,0:T(8,128)S(1)} %select_maximum_fusion.2, pred[256,512]{0,1:T(8,128)(4,1)S(1)} %compare_and_fusion.2), kind=kLoop, calls=%fused_computation.7.clone.1 | loop fusion | flops 14672896 | bytes 14868480 | tf_op jit(solution)/shard_map/while/body/eval_jaxpr/reduce_sum | solution.py:92
  466.5 8.0 %fusion.64 = f32[4,7,256,128]{3,2,1,0:T(8,128)S(1)} fusion(f32[4,7,256,128]{3,2,1,0:T(8,128)S(1)} %copy-done.2, bf16[512,4,128,1]{0,2,3,1:T(8,128)(2,1)S(1)} %bitcast.143, f32[4,512,256,7]{2,1,3,0:T(8,128)} %get-tuple-element.238, f32[4,7,256]{2,1,0:T(8,128)S(1)} %select_maximum_fusion.2, pred[256,512]{0,1:T(8,128)(4,1)S(1)} %compare_and_fusion.2, ...), kind=kOutput, calls=%fused_computation.11.clone.1 | convolution fusion | flops 956956672 | bytes 22732800 | tf_op jit(solution)/shard_map/while/body/eval_jaxpr/ghrn,ngo->ghro/dot_general | solution.py:93
  474.5 1.9 copy-done.3
  477.8 1.3 constant_dynamic-slice_fusion.2
  479.8 1.4 copy-done
  481.2 6.5 %fusion.61 = (f32[4,7,256]{2,1,0:T(8,128)S(1)}, f32[4,512,256,7]{2,1,3,0:T(8,128)}) fusion(pred[256,512]{0,1:T(8,128)(4,1)S(1)} %compare_and_fusion.2, bf16[512,4,128,1]{0,2,3,1:T(8,128)(2,1)S(1)} %bitcast.141, bf16[256,4,7,128]{3,0,2,1:T(8,128)(2,1)S(1)} %copy-done), kind=kOutput, calls=%fused_computation.3.clone.1 | convolution fusion | flops 950526976 | bytes 17199104 | tf_op jit(solution)/shard_map/while/body/eval_jaxpr/rgho,ngo->ghrn/dot_general | solution.py:83
  487.7 8.3 %fusion.62 = f32[4,7,256]{2,1,0:T(8,128)S(1)} fusion(f32[4,512,256,7]{2,1,3,0:T(8,128)} %get-tuple-element.238, f32[4,7,256]{2,1,0:T(8,128)S(1)} %select_maximum_fusion.2, pred[256,512]{0,1:T(8,128)(4,1)S(1)} %compare_and_fusion.2), kind=kLoop, calls=%fused_computation.7.clone.1 | loop fusion | flops 14672896 | bytes 14868480 | tf_op jit(solution)/shard_map/while/body/eval_jaxpr/reduce_sum | solution.py:92
  496.1 8.0 %fusion.64 = f32[4,7,256,128]{3,2,1,0:T(8,128)S(1)} fusion(f32[4,7,256,128]{3,2,1,0:T(8,128)S(1)} %copy-done.2, bf16[512,4,128,1]{0,2,3,1:T(8,128)(2,1)S(1)} %bitcast.143, f32[4,512,256,7]{2,1,3,0:T(8,128)} %get-tuple-element.238, f32[4,7,256]{2,1,0:T(8,128)S(1)} %select_maximum_fusion.2, pred[256,512]{0,1:T(8,128)(4,1)S(1)} %compare_and_fusion.2, ...), kind=kOutput, calls=%fused_computation.11.clone.1 | convolution fusion | flops 956956672 | bytes 22732800 | tf_op jit(solution)/shard_map/while/body/eval_jaxpr/ghrn,ngo->ghro/dot_general | solution.py:93
  504.1 1.9 copy-done.3
  509.4 1.4 copy-done
  510.8 6.5 %fusion.61 = (f32[4,7,256]{2,1,0:T(8,128)S(1)}, f32[4,512,256,7]{2,1,3,0:T(8,128)}) fusion(pred[256,512]{0,1:T(8,128)(4,1)S(1)} %compare_and_fusion.2, bf16[512,4,128,1]{0,2,3,1:T(8,128)(2,1)S(1)} %bitcast.141, bf16[256,4,7,128]{3,0,2,1:T(8,128)(2,1)S(1)} %copy-done), kind=kOutput, calls=%fused_computation.3.clone.1 | convolution fusion | flops 950526976 | bytes 17199104 | tf_op jit(solution)/shard_map/while/body/eval_jaxpr/rgho,ngo->ghrn/dot_general | solution.py:83
  517.3 8.3 %fusion.62 = f32[4,7,256]{2,1,0:T(8,128)S(1)} fusion(f32[4,512,256,7]{2,1,3,0:T(8,128)} %get-tuple-element.238, f32[4,7,256]{2,1,0:T(8,128)S(1)} %select_maximum_fusion.2, pred[256,512]{0,1:T(8,128)(4,1)S(1)} %compare_and_fusion.2), kind=kLoop, calls=%fused_computation.7.clone.1 | loop fusion | flops 14672896 | bytes 14868480 | tf_op jit(solution)/shard_map/while/body/eval_jaxpr/reduce_sum | solution.py:92
  525.6 8.0 %fusion.64 = f32[4,7,256,128]{3,2,1,0:T(8,128)S(1)} fusion(f32[4,7,256,128]{3,2,1,0:T(8,128)S(1)} %copy-done.2, bf16[512,4,128,1]{0,2,3,1:T(8,128)(2,1)S(1)} %bitcast.143, f32[4,512,256,7]{2,1,3,0:T(8,128)} %get-tuple-element.238, f32[4,7,256]{2,1,0:T(8,128)S(1)} %select_maximum_fusion.2, pred[256,512]{0,1:T(8,128)(4,1)S(1)} %compare_and_fusion.2, ...), kind=kOutput, calls=%fused_computation.11.clone.1 | convolution fusion | flops 956956672 | bytes 22732800 | tf_op jit(solution)/shard_map/while/body/eval_jaxpr/ghrn,ngo->ghro/dot_general | solution.py:93
  533.7 1.9 copy-done.3
  538.9 1.4 copy-done
  540.4 6.5 %fusion.61 = (f32[4,7,256]{2,1,0:T(8,128)S(1)}, f32[4,512,256,7]{2,1,3,0:T(8,128)}) fusion(pred[256,512]{0,1:T(8,128)(4,1)S(1)} %compare_and_fusion.2, bf16[512,4,128,1]{0,2,3,1:T(8,128)(2,1)S(1)} %bitcast.141, bf16[256,4,7,128]{3,0,2,1:T(8,128)(2,1)S(1)} %copy-done), kind=kOutput, calls=%fused_computation.3.clone.1 | convolution fusion | flops 950526976 | bytes 17199104 | tf_op jit(solution)/shard_map/while/body/eval_jaxpr/rgho,ngo->ghrn/dot_general | solution.py:83
  546.9 8.3 %fusion.62 = f32[4,7,256]{2,1,0:T(8,128)S(1)} fusion(f32[4,512,256,7]{2,1,3,0:T(8,128)} %get-tuple-element.238, f32[4,7,256]{2,1,0:T(8,128)S(1)} %select_maximum_fusion.2, pred[256,512]{0,1:T(8,128)(4,1)S(1)} %compare_and_fusion.2), kind=kLoop, calls=%fused_computation.7.clone.1 | loop fusion | flops 14672896 | bytes 14868480 | tf_op jit(solution)/shard_map/while/body/eval_jaxpr/reduce_sum | solution.py:92
  555.2 8.0 %fusion.64 = f32[4,7,256,128]{3,2,1,0:T(8,128)S(1)} fusion(f32[4,7,256,128]{3,2,1,0:T(8,128)S(1)} %copy-done.2, bf16[512,4,128,1]{0,2,3,1:T(8,128)(2,1)S(1)} %bitcast.143, f32[4,512,256,7]{2,1,3,0:T(8,128)} %get-tuple-element.238, f32[4,7,256]{2,1,0:T(8,128)S(1)} %select_maximum_fusion.2, pred[256,512]{0,1:T(8,128)(4,1)S(1)} %compare_and_fusion.2, ...), kind=kOutput, calls=%fused_computation.11.clone.1 | convolution fusion | flops 956956672 | bytes 22732800 | tf_op jit(solution)/shard_map/while/body/eval_jaxpr/ghrn,ngo->ghro/dot_general | solution.py:93
  563.3 1.9 copy-done.3
  568.5 1.4 copy-done
  569.9 6.5 %fusion.61 = (f32[4,7,256]{2,1,0:T(8,128)S(1)}, f32[4,512,256,7]{2,1,3,0:T(8,128)}) fusion(pred[256,512]{0,1:T(8,128)(4,1)S(1)} %compare_and_fusion.2, bf16[512,4,128,1]{0,2,3,1:T(8,128)(2,1)S(1)} %bitcast.141, bf16[256,4,7,128]{3,0,2,1:T(8,128)(2,1)S(1)} %copy-done), kind=kOutput, calls=%fused_computation.3.clone.1 | convolution fusion | flops 950526976 | bytes 17199104 | tf_op jit(solution)/shard_map/while/body/eval_jaxpr/rgho,ngo->ghrn/dot_general | solution.py:83
  576.5 8.3 %fusion.62 = f32[4,7,256]{2,1,0:T(8,128)S(1)} fusion(f32[4,512,256,7]{2,1,3,0:T(8,128)} %get-tuple-element.238, f32[4,7,256]{2,1,0:T(8,128)S(1)} %select_maximum_fusion.2, pred[256,512]{0,1:T(8,128)(4,1)S(1)} %compare_and_fusion.2), kind=kLoop, calls=%fused_computation.7.clone.1 | loop fusion | flops 14672896 | bytes 14868480 | tf_op jit(solution)/shard_map/while/body/eval_jaxpr/reduce_sum | solution.py:92
  584.8 8.0 %fusion.64 = f32[4,7,256,128]{3,2,1,0:T(8,128)S(1)} fusion(f32[4,7,256,128]{3,2,1,0:T(8,128)S(1)} %copy-done.2, bf16[512,4,128,1]{0,2,3,1:T(8,128)(2,1)S(1)} %bitcast.143, f32[4,512,256,7]{2,1,3,0:T(8,128)} %get-tuple-element.238, f32[4,7,256]{2,1,0:T(8,128)S(1)} %select_maximum_fusion.2, pred[256,512]{0,1:T(8,128)(4,1)S(1)} %compare_and_fusion.2, ...), kind=kOutput, calls=%fused_computation.11.clone.1 | convolution fusion | flops 956956672 | bytes 22732800 | tf_op jit(solution)/shard_map/while/body/eval_jaxpr/ghrn,ngo->ghro/dot_general | solution.py:93
  592.9 1.9 copy-done.3
  594.7 4.6 copy.48
  599.3 2.5 divide_convert_fusion
  601.8 2.6 copy.49
  (165 shorter events, 41.1 us)
Async XLA Ops:
  7.2 2.7 copy-start.1
  7.2 30.8 %all-gather.9.cloned.1.call-start = ((), (), s32[]{:S(2)}) async-start(), calls=%async_computation.3 | async-start | bytes 2654208 | tf_op jit(solution)/shard_map/all_gather | solution.py:43
  7.9 208.7 %all-gather.5.cloned.1.call-start = ((), (), s32[]{:S(2)}) async-start(), calls=%async_computation.1 | async-start | bytes 31195136 | tf_op jit(solution)/shard_map/all_gather | solution.py:40
  242.1 5.5 copy-start.5
  242.1 40.6 %all-to-all-start = ((bf16[16,256,288]{1,2,0:T(8,128)(2,1)}), bf16[16,256,288]{1,2,0:T(8,128)(2,1)S(1)}, u32[]{:S(2)}, u32[]{:S(2)}) async-start(bf16[16,256,288]{1,2,0:T(8,128)(2,1)} %fusion.20), calls=%async_computation | async-start | bytes 4718592 | tf_op jit(solution)/shard_map/all_to_all | solution.py:50
  247.5 110.5 %all-gather.7.cloned.1.call-start = ((), (), s32[]{:S(2)}) async-start(), calls=%async_computation.2 | async-start | bytes 8912896 | tf_op jit(solution)/shard_map/all_gather | solution.py:109
  294.6 2.5 copy-start.4
  361.4 1.5 copy-start
  369.4 8.4 %copy-start.2 = (f32[4,7,256,128]{3,2,1,0:T(8,128)S(1)}, f32[4,7,256,128]{3,2,1,0:T(8,128)}, u32[]{:S(2)}) copy-start(f32[4,7,256,128]{3,2,1,0:T(8,128)} %get-tuple-element.257) | copy-start | bytes 11010052 | tf_op jit(solution)/shard_map/while
  385.8 1.9 copy-start.3
  390.9 1.5 copy-start
  399.0 8.4 %copy-start.2 = (f32[4,7,256,128]{3,2,1,0:T(8,128)S(1)}, f32[4,7,256,128]{3,2,1,0:T(8,128)}, u32[]{:S(2)}) copy-start(f32[4,7,256,128]{3,2,1,0:T(8,128)} %get-tuple-element.257) | copy-start | bytes 11010052 | tf_op jit(solution)/shard_map/while
  415.4 1.9 copy-start.3
  420.5 1.5 copy-start
  428.5 8.4 %copy-start.2 = (f32[4,7,256,128]{3,2,1,0:T(8,128)S(1)}, f32[4,7,256,128]{3,2,1,0:T(8,128)}, u32[]{:S(2)}) copy-start(f32[4,7,256,128]{3,2,1,0:T(8,128)} %get-tuple-element.257) | copy-start | bytes 11010052 | tf_op jit(solution)/shard_map/while
  444.9 1.9 copy-start.3
  450.1 1.5 copy-start
  458.1 8.4 %copy-start.2 = (f32[4,7,256,128]{3,2,1,0:T(8,128)S(1)}, f32[4,7,256,128]{3,2,1,0:T(8,128)}, u32[]{:S(2)}) copy-start(f32[4,7,256,128]{3,2,1,0:T(8,128)} %get-tuple-element.257) | copy-start | bytes 11010052 | tf_op jit(solution)/shard_map/while
  474.5 1.9 copy-start.3
  479.7 1.5 copy-start
  487.7 8.4 %copy-start.2 = (f32[4,7,256,128]{3,2,1,0:T(8,128)S(1)}, f32[4,7,256,128]{3,2,1,0:T(8,128)}, u32[]{:S(2)}) copy-start(f32[4,7,256,128]{3,2,1,0:T(8,128)} %get-tuple-element.257) | copy-start | bytes 11010052 | tf_op jit(solution)/shard_map/while
  504.1 1.9 copy-start.3
  509.3 1.5 copy-start
  517.3 8.4 %copy-start.2 = (f32[4,7,256,128]{3,2,1,0:T(8,128)S(1)}, f32[4,7,256,128]{3,2,1,0:T(8,128)}, u32[]{:S(2)}) copy-start(f32[4,7,256,128]{3,2,1,0:T(8,128)} %get-tuple-element.257) | copy-start | bytes 11010052 | tf_op jit(solution)/shard_map/while
  533.7 1.9 copy-start.3
  538.9 1.5 copy-start
  546.9 8.4 %copy-start.2 = (f32[4,7,256,128]{3,2,1,0:T(8,128)S(1)}, f32[4,7,256,128]{3,2,1,0:T(8,128)}, u32[]{:S(2)}) copy-start(f32[4,7,256,128]{3,2,1,0:T(8,128)} %get-tuple-element.257) | copy-start | bytes 11010052 | tf_op jit(solution)/shard_map/while
  563.3 1.9 copy-start.3
  568.4 1.5 copy-start
  576.5 8.4 %copy-start.2 = (f32[4,7,256,128]{3,2,1,0:T(8,128)S(1)}, f32[4,7,256,128]{3,2,1,0:T(8,128)}, u32[]{:S(2)}) copy-start(f32[4,7,256,128]{3,2,1,0:T(8,128)} %get-tuple-element.257) | copy-start | bytes 11010052 | tf_op jit(solution)/shard_map/while
  592.9 1.9 copy-start.3
Sparse Core Ops, SparseCore 0:
  9.7 28.2 all-gather.8
  40.7 175.8 all-gather.4
  289.4 68.6 all-gather.6
